TPU v7x, 128 devices: a whole 4x4x4 slice. The times are simulated.
128 devices in a mesh: row: 16 (over x, y_hi, core), col: 8 (over z, y_lo).
Axes of the slice: x: 4, y: 4 (y_hi: 2, y_lo: 2; y = y_hi * 2 + y_lo), z: 4, core: 2. Of those that a mesh axis runs over, the one named last changes fastest.
Arguments:
- band_cells: float32 [3, 1024, 2], P(None, ('row', 'col')), may hold values from 0 to 1
- cell_counts: int32 [1024], P(('row', 'col')), may hold values from 1 to 2, as said below
- cell_assign: int32 [1024], P(('row', 'col')), may hold values from 0 to 1023, as said below
- wake_pos: float32 [3, 1048576], P(None, ('row', 'col')), may hold values from 0 to 1
- wake_strength: float32 [3, 1048576], P(None, ('row', 'col')), may hold values from -0.005859375 to 0.005859375
- wake_core: float32 [1, 1048576], P(None, ('row', 'col')), may hold values from 0.05 to 0.15
Outputs:
- velocity: float32 [3, 1024, 2], P(None, ('row', 'col'))
- gradient: float32 [9, 1024, 2], P(None, ('row', 'col'))
Inputs may be any that keep to these rules, and one draw needn't show every extreme that they name: `cell_counts`: each band cell holds its live particles in its first slots; some cell is full in every draw. `cell_assign`: A permutation of the cells. The cells of the device with index d along row+col go to positions q with q // 64 == d // 8; at most 1 of them land in the positions of any one device (q // 8); where 8 is a multiple of 8, exactly 1 land in the positions of each device of the group, else some pair of devices reaches 1.
All inputs are finite; a program needn't handle non-finite values.
Results may differ from a plain program's by a relative error of at most 0.0003.
Values sent between devices are 32-bit elements; how exact they have to be, the bound alone decides.
No kernel may reach another device: no remote copies, remote signals or barrier semaphores. Data moves between devices by JAX's collectives and lax.ppermute only.
A program may use at most 64 MiB of HBM per device.

v0:
```python
import math
import jax
import jax.numpy as jnp
from jax import lax
from jax.sharding import PartitionSpec as P

HIGHEST = lax.Precision.HIGHEST


def block_sums(target_pos, source_pos, source_str, source_core):
    delta_x = target_pos[0][:, None] - source_pos[0][None, :]
    delta_y = target_pos[1][:, None] - source_pos[1][None, :]
    delta_z = target_pos[2][:, None] - source_pos[2][None, :]
    radius_sq = (
        delta_x * delta_x
        + delta_y * delta_y
        + delta_z * delta_z
        + source_core[0][None, :] * source_core[0][None, :]
    )
    inverse = lax.rsqrt(radius_sq)
    kernel_three = inverse * inverse * inverse
    kernel_five = kernel_three * inverse * inverse
    alpha_x = source_str[0][None, :]
    alpha_y = source_str[1][None, :]
    alpha_z = source_str[2][None, :]
    cross_x = delta_y * alpha_z - delta_z * alpha_y
    cross_y = delta_z * alpha_x - delta_x * alpha_z
    cross_z = delta_x * alpha_y - delta_y * alpha_x
    terms_list = [
        kernel_three * cross_x,
        kernel_three * cross_y,
        kernel_three * cross_z,
        kernel_three * alpha_x,
        kernel_three * alpha_y,
        kernel_three * alpha_z,
    ]
    for along in (delta_x, delta_y, delta_z):
        for cross in (cross_x, cross_y, cross_z):
            terms_list.append(kernel_five * along * cross)
    return jnp.stack([jnp.sum(term, axis=1) for term in terms_list])


def pair_sums(target_pos, source_pos, source_str, source_core):
    source_total = source_pos.shape[1]
    block_width = math.gcd(source_total, max(512, 1048576 // target_pos.shape[1]))
    block_steps = source_total // block_width

    def one_block(running, block_index):
        offset = block_index * block_width
        part_pos = lax.dynamic_slice_in_dim(source_pos, offset, block_width, 1)
        part_str = lax.dynamic_slice_in_dim(source_str, offset, block_width, 1)
        part_core = lax.dynamic_slice_in_dim(source_core, offset, block_width, 1)
        return (running + block_sums(target_pos, part_pos, part_str, part_core), None)

    start_sums = jnp.zeros((15, target_pos.shape[1]), jnp.float32)
    running, unused = lax.scan(one_block, start_sums, jnp.arange(block_steps, dtype=jnp.int32))
    return running


def combine_rows(kernel_sums):
    biot_scale = -1.0 / (4.0 * math.pi)
    swirl_x, swirl_y, swirl_z = (kernel_sums[3], kernel_sums[4], kernel_sums[5])
    zero_row = jnp.zeros_like(swirl_x)
    levi_terms = [
        [zero_row, swirl_z, -swirl_y],
        [-swirl_z, zero_row, swirl_x],
        [swirl_y, -swirl_x, zero_row],
    ]
    out_rows = [
        biot_scale * kernel_sums[0],
        biot_scale * kernel_sums[1],
        biot_scale * kernel_sums[2],
    ]
    for comp_m in range(3):
        for comp_n in range(3):
            out_rows.append(
                biot_scale
                * (levi_terms[comp_m][comp_n] - 3.0 * kernel_sums[6 + comp_n * 3 + comp_m])
            )
    return jnp.stack(out_rows)


def apply_mask(finished_rows, slot_counts, slot_cap):
    slot_ids = jnp.arange(slot_cap).astype(slot_counts.dtype)
    alive_mask = (slot_ids[None, :] < slot_counts[:, None]).astype(jnp.float32).reshape(-1)
    masked = finished_rows * alive_mask[None, :]
    cell_total = slot_counts.shape[0]
    return (
        masked[0:3].reshape(3, cell_total, slot_cap),
        masked[3:12].reshape(9, cell_total, slot_cap),
    )


def per_device(band_cells, cell_counts, cell_assign, wake_pos, wake_strength, wake_core):
    axes = ("row", "col")
    col_devs = lax.axis_size("col")
    cell_total = band_cells.shape[1]
    slot_cap = band_cells.shape[2]
    group_cells = cell_total * col_devs
    packed = jnp.concatenate(
        [
            band_cells.transpose(1, 0, 2).reshape(cell_total, 3 * slot_cap),
            cell_counts.astype(jnp.float32)[:, None],
            cell_assign.astype(jnp.float32)[:, None],
        ],
        axis=1,
    )
    every_cell = lax.all_gather(packed, axes, axis=0, tiled=True)
    all_cells = every_cell.shape[0]
    groups = all_cells // group_cells
    grouped = every_cell.reshape(groups, group_cells, 3 * slot_cap + 2)
    within = grouped[:, :, -1].astype(jnp.int32) % group_cells
    position = jnp.arange(group_cells, dtype=jnp.int32)
    chosen = within[:, None, :] == position[None, :, None]
    relaid = jnp.sum(
        jnp.where(chosen[:, :, :, None], grouped[:, None, :, : 3 * slot_cap + 1], 0.0), axis=2
    ).reshape(all_cells, 3 * slot_cap + 1)
    target_pos = relaid[:, : 3 * slot_cap].reshape(all_cells, 3, slot_cap)
    target_pos = target_pos.transpose(1, 0, 2).reshape(3, all_cells * slot_cap)
    device = lax.axis_index("row") * col_devs + lax.axis_index("col")
    own_counts = lax.dynamic_slice_in_dim(relaid[:, 3 * slot_cap], device * cell_total, cell_total)
    local_sums = pair_sums(target_pos, wake_pos, wake_strength, wake_core)
    own_rows = lax.psum_scatter(local_sums, axes, scatter_dimension=1, tiled=True)
    finished_rows = combine_rows(own_rows)
    return apply_mask(finished_rows, own_counts, slot_cap)


def solution(mesh):
    placed = (
        P(None, ("row", "col"), None),
        P(("row", "col")),
        P(("row", "col")),
        P(None, ("row", "col")),
        P(None, ("row", "col")),
        P(None, ("row", "col")),
    )
    return jax.shard_map(
        per_device,
        mesh=mesh,
        in_specs=placed,
        out_specs=(P(None, ("row", "col"), None), P(None, ("row", "col"), None)),
        check_vma=False,
    )
```

profile of v0, /device:TPU:0, one launch (start us, length us, event | category | flops | bytes accessed | tf_op | source)
XLA Modules:
  0.0 1217.7 jit_solution(9751047633105874884)
XLA Ops:
  8.7 320.8 %all_gather.3 = f32[1024,8]{1,0:T(8,128)S(1)} all-gather(f32[8,8]{1,0:T(8,128)S(1)} %copy.62), channel_id=1, replica_groups=mesh['row'=16,'col'=8] {'row','col'}, dimensions={0}, use_global_device_ids=true | all-gather | bytes 33024 | tf_op jit(solution)/shard_map/all_gather | solution.py:108
  330.2 1.0 select_reduce_fusion
  332.8 240.7 %while.11 = (s32[]{:T(128)}, f32[15,2048]{1,0:T(8,128)S(1)}, f32[3,2048]{1,0:T(4,128)S(1)}, s32[16]{0:T(128)S(1)}, f32[3,8192]{1,0:T(4,128)}, /*index=5*/f32[1,8...) while((s32[]{:T(128)}, f32[15,2048]{1,0:T(8,128)S(1)}, ...), condition=%wide.region_17.18_spmd.clone, body=%wide.region_1.17_spmd.clone.sunk | while | flops 57702920 | bytes 854257 | solution.py:56
  335.9 11.7 fusion.57
  350.9 11.7 fusion.57
  365.9 11.7 fusion.57
  381.0 11.7 fusion.57
  394.2 0.9 constant_dynamic-slice_fusion.3
  396.0 11.7 fusion.57
  411.1 11.7 fusion.57
  426.1 11.7 fusion.57
  441.2 11.7 fusion.57
  454.4 0.9 constant_dynamic-slice_fusion.3
  456.2 11.7 fusion.57
  471.2 11.7 fusion.57
  486.3 11.7 fusion.57
  501.3 11.7 fusion.57
  516.4 11.7 fusion.57
  531.4 11.7 fusion.57
  546.5 11.7 fusion.57
  561.5 11.7 fusion.57
  573.5 1.4 copy.84
  575.1 632.5 %reduce-scatter.4.cloned.1.call-done = f32[16,15]{1,0:T(8,128)} async-done(((f32[2048,15]{1,0:T(8,128)}), f32[16,15]{1,0:T(8,128)}) %reduce-scatter.4.cloned.1.call-update) | async-done | bytes 976
  1207.6 1.7 fusion.33
  (121 shorter events, 45.8 us)
Async XLA Ops:
  7.2 1200.5 %reduce-scatter.4.cloned.1.call-start = ((), (), s32[]{:S(2)}) async-start(), calls=%async_computation.1 | async-start | bytes 1056768
Sparse Core Ops, SparseCore 0:
  575.0 632.5 reduce-scatter.3
where the time goes:
time: 1220 us
  waiting for transfers between devices  633 us (52%)
  blocking collectives  321 us (26%)
  other arithmetic  206 us (17%)
  local copies, waits for them, and re-layouts  33 us (3%)
  between operations  14.1 us (1%)
    unnamed x2, waiting for transfers between devices  633 us
    all_gather x1, blocking collectives, per_device(): every_cell = lax.all_gather(packed, axes, axis=0, tiled=True)  321 us
    reduce_sum x16, other arithmetic, block_sums(): return jnp.stack([jnp.sum(term, axis=1) for term in terms_list])  187 us
  transfers between devices with their start and end apart: 1, of which 1 were waited for; matrix products, arithmetic and copies ran while one was open for 0% of the time, Pallas kernels for 0%

commit v1 on v0

--- a/solution.py
+++ b/solution.py
@@ -105,7 +105,9 @@
         ],
         axis=1,
     )
-    every_cell = lax.all_gather(packed, axes, axis=0, tiled=True)
+    every_cell = jnp.concatenate(
+        lax.all_to_all(jnp.stack([packed] * lax.axis_size(axes)), axes, 0, 0), axis=0
+    )
     all_cells = every_cell.shape[0]
     groups = all_cells // group_cells
     grouped = every_cell.reshape(groups, group_cells, 3 * slot_cap + 2)

time: 1220 us -> 926 us (0.76)
  blocking collectives: 321 us -> 0 us
  waiting for transfers between devices: 633 us -> 648 us
    all_gather x1 -> x0, blocking collectives: 321 us -> none  [per_device(): every_cell = lax.all_gather(packed, axes, axis=0, tiled=True)]
    all_to_all x0 -> x1, waiting for transfers between devices: none -> 13.7 us  [per_device(): lax.all_to_all(jnp.stack([packed] * lax.axis_size(axes)), axes, 0, 0)]
  transfers between devices with their start and end apart: 1 -> 2, of which waited for: 1 -> 2; matrix products, arithmetic and copies ran while one was open for 0% -> 0% of each run, Pallas kernels for 0% -> 0%
where the time goes in v1:
time: 926 us; the launch traced here: 924 us
  waiting for transfers between devices  648 us (70%)
  other arithmetic  206 us (22%)
  local copies, waits for them, and re-layouts  33.5 us (4%)
  between operations  14.1 us (2%)
  starting transfers between devices  11.2 us (1%)
  loops' own time  11.1 us (1%)
    unnamed x2, waiting for transfers between devices  635 us
    reduce_sum x16, other arithmetic, block_sums(): return jnp.stack([jnp.sum(term, axis=1) for term in terms_list])  187 us
  transfers between devices with their start and end apart: 2, of which 2 were waited for; matrix products, arithmetic and copies ran while one was open for 0% of the time, Pallas kernels for 0%

profile of v1, /device:TPU:0, one launch (start us, length us, event | category | flops | bytes accessed | tf_op | source)
XLA Modules:
  0.0 924.3 jit_solution(3807354312942650091)
XLA Ops:
  9.4 11.1 %all-to-all-start = ((f32[128,8,8]{1,2,0:T(8,128)}), f32[128,8,8]{1,2,0:T(8,128)S(1)}, u32[]{:S(2)}, u32[]{:S(2)}) async-start(f32[128,8,8]{1,2,0:T(8,128)} %stack.36), calls=%async_computation | async-start | bytes 1048576 | tf_op jit(solution)/shard_map/all_to_all | solution.py:109
  20.6 13.7 %all-to-all-done = f32[128,8,8]{1,2,0:T(8,128)S(1)} async-done(((f32[128,8,8]{1,2,0:T(8,128)}), f32[128,8,8]{1,2,0:T(8,128)S(1)}, u32[]{:S(2)}, u32[]{:S(2)}) %all-to-all-start) | async-done | bytes 32800 | tf_op jit(solution)/shard_map/all_to_all | solution.py:109
  34.7 1.0 select_reduce_fusion
  37.3 240.7 %while.11 = (s32[]{:T(128)}, f32[15,2048]{1,0:T(8,128)S(1)}, f32[3,2048]{1,0:T(4,128)S(1)}, s32[16]{0:T(128)S(1)}, f32[3,8192]{1,0:T(4,128)}, /*index=5*/f32[1,8...) while((s32[]{:T(128)}, f32[15,2048]{1,0:T(8,128)S(1)}, ...), condition=%wide.region_17.18_spmd.clone, body=%wide.region_1.17_spmd.clone.sunk | while | flops 57702920 | bytes 854257 | solution.py:56
  40.4 11.7 %fusion.58 = (f32[2048]{0:T(1024)S(1)}, f32[2048]{0:T(1024)S(1)}, f32[2048]{0:T(1024)S(1)}, f32[2048]{0:T(1024)S(1)}, f32[2048]{0:T(1024)S(1)}, /*index=5*/f32[2...) fusion(f32[512]{0:T(512)S(1)} %bitcast.135, ...), kind=kLoop, calls=%fused_computation.28.clone.1 | loop fusion | flops 57640960 | bytes 161792 | tf_op jit(solution)/shard_map/while/body/eval_jaxpr/reduce_sum | solution.py:40
  55.4 11.7 %fusion.58 = (f32[2048]{0:T(1024)S(1)}, f32[2048]{0:T(1024)S(1)}, f32[2048]{0:T(1024)S(1)}, f32[2048]{0:T(1024)S(1)}, f32[2048]{0:T(1024)S(1)}, /*index=5*/f32[2...) fusion(f32[512]{0:T(512)S(1)} %bitcast.135, ...), kind=kLoop, calls=%fused_computation.28.clone.1 | loop fusion | flops 57640960 | bytes 161792 | tf_op jit(solution)/shard_map/while/body/eval_jaxpr/reduce_sum | solution.py:40
  70.4 11.7 %fusion.58 = (f32[2048]{0:T(1024)S(1)}, f32[2048]{0:T(1024)S(1)}, f32[2048]{0:T(1024)S(1)}, f32[2048]{0:T(1024)S(1)}, f32[2048]{0:T(1024)S(1)}, /*index=5*/f32[2...) fusion(f32[512]{0:T(512)S(1)} %bitcast.135, ...), kind=kLoop, calls=%fused_computation.28.clone.1 | loop fusion | flops 57640960 | bytes 161792 | tf_op jit(solution)/shard_map/while/body/eval_jaxpr/reduce_sum | solution.py:40
  85.5 11.7 %fusion.58 = (f32[2048]{0:T(1024)S(1)}, f32[2048]{0:T(1024)S(1)}, f32[2048]{0:T(1024)S(1)}, f32[2048]{0:T(1024)S(1)}, f32[2048]{0:T(1024)S(1)}, /*index=5*/f32[2...) fusion(f32[512]{0:T(512)S(1)} %bitcast.135, ...), kind=kLoop, calls=%fused_computation.28.clone.1 | loop fusion | flops 57640960 | bytes 161792 | tf_op jit(solution)/shard_map/while/body/eval_jaxpr/reduce_sum | solution.py:40
  100.5 11.7 %fusion.58 = (f32[2048]{0:T(1024)S(1)}, f32[2048]{0:T(1024)S(1)}, f32[2048]{0:T(1024)S(1)}, f32[2048]{0:T(1024)S(1)}, f32[2048]{0:T(1024)S(1)}, /*index=5*/f32[2...) fusion(f32[512]{0:T(512)S(1)} %bitcast.135, ...), kind=kLoop, calls=%fused_computation.28.clone.1 | loop fusion | flops 57640960 | bytes 161792 | tf_op jit(solution)/shard_map/while/body/eval_jaxpr/reduce_sum | solution.py:40
  115.6 11.7 %fusion.58 = (f32[2048]{0:T(1024)S(1)}, f32[2048]{0:T(1024)S(1)}, f32[2048]{0:T(1024)S(1)}, f32[2048]{0:T(1024)S(1)}, f32[2048]{0:T(1024)S(1)}, /*index=5*/f32[2...) fusion(f32[512]{0:T(512)S(1)} %bitcast.135, ...), kind=kLoop, calls=%fused_computation.28.clone.1 | loop fusion | flops 57640960 | bytes 161792 | tf_op jit(solution)/shard_map/while/body/eval_jaxpr/reduce_sum | solution.py:40
  130.6 11.7 %fusion.58 = (f32[2048]{0:T(1024)S(1)}, f32[2048]{0:T(1024)S(1)}, f32[2048]{0:T(1024)S(1)}, f32[2048]{0:T(1024)S(1)}, f32[2048]{0:T(1024)S(1)}, /*index=5*/f32[2...) fusion(f32[512]{0:T(512)S(1)} %bitcast.135, ...), kind=kLoop, calls=%fused_computation.28.clone.1 | loop fusion | flops 57640960 | bytes 161792 | tf_op jit(solution)/shard_map/while/body/eval_jaxpr/reduce_sum | solution.py:40
  143.8 0.9 constant_dynamic-slice_fusion.3
  145.7 11.7 %fusion.58 = (f32[2048]{0:T(1024)S(1)}, f32[2048]{0:T(1024)S(1)}, f32[2048]{0:T(1024)S(1)}, f32[2048]{0:T(1024)S(1)}, f32[2048]{0:T(1024)S(1)}, /*index=5*/f32[2...) fusion(f32[512]{0:T(512)S(1)} %bitcast.135, ...), kind=kLoop, calls=%fused_computation.28.clone.1 | loop fusion | flops 57640960 | bytes 161792 | tf_op jit(solution)/shard_map/while/body/eval_jaxpr/reduce_sum | solution.py:40
  160.7 11.7 %fusion.58 = (f32[2048]{0:T(1024)S(1)}, f32[2048]{0:T(1024)S(1)}, f32[2048]{0:T(1024)S(1)}, f32[2048]{0:T(1024)S(1)}, f32[2048]{0:T(1024)S(1)}, /*index=5*/f32[2...) fusion(f32[512]{0:T(512)S(1)} %bitcast.135, ...), kind=kLoop, calls=%fused_computation.28.clone.1 | loop fusion | flops 57640960 | bytes 161792 | tf_op jit(solution)/shard_map/while/body/eval_jaxpr/reduce_sum | solution.py:40
  175.7 11.7 %fusion.58 = (f32[2048]{0:T(1024)S(1)}, f32[2048]{0:T(1024)S(1)}, f32[2048]{0:T(1024)S(1)}, f32[2048]{0:T(1024)S(1)}, f32[2048]{0:T(1024)S(1)}, /*index=5*/f32[2...) fusion(f32[512]{0:T(512)S(1)} %bitcast.135, ...), kind=kLoop, calls=%fused_computation.28.clone.1 | loop fusion | flops 57640960 | bytes 161792 | tf_op jit(solution)/shard_map/while/body/eval_jaxpr/reduce_sum | solution.py:40
  190.8 11.7 %fusion.58 = (f32[2048]{0:T(1024)S(1)}, f32[2048]{0:T(1024)S(1)}, f32[2048]{0:T(1024)S(1)}, f32[2048]{0:T(1024)S(1)}, f32[2048]{0:T(1024)S(1)}, /*index=5*/f32[2...) fusion(f32[512]{0:T(512)S(1)} %bitcast.135, ...), kind=kLoop, calls=%fused_computation.28.clone.1 | loop fusion | flops 57640960 | bytes 161792 | tf_op jit(solution)/shard_map/while/body/eval_jaxpr/reduce_sum | solution.py:40
  205.8 11.7 %fusion.58 = (f32[2048]{0:T(1024)S(1)}, f32[2048]{0:T(1024)S(1)}, f32[2048]{0:T(1024)S(1)}, f32[2048]{0:T(1024)S(1)}, f32[2048]{0:T(1024)S(1)}, /*index=5*/f32[2...) fusion(f32[512]{0:T(512)S(1)} %bitcast.135, ...), kind=kLoop, calls=%fused_computation.28.clone.1 | loop fusion | flops 57640960 | bytes 161792 | tf_op jit(solution)/shard_map/while/body/eval_jaxpr/reduce_sum | solution.py:40
  220.9 11.7 %fusion.58 = (f32[2048]{0:T(1024)S(1)}, f32[2048]{0:T(1024)S(1)}, f32[2048]{0:T(1024)S(1)}, f32[2048]{0:T(1024)S(1)}, f32[2048]{0:T(1024)S(1)}, /*index=5*/f32[2...) fusion(f32[512]{0:T(512)S(1)} %bitcast.135, ...), kind=kLoop, calls=%fused_computation.28.clone.1 | loop fusion | flops 57640960 | bytes 161792 | tf_op jit(solution)/shard_map/while/body/eval_jaxpr/reduce_sum | solution.py:40
  235.9 11.7 %fusion.58 = (f32[2048]{0:T(1024)S(1)}, f32[2048]{0:T(1024)S(1)}, f32[2048]{0:T(1024)S(1)}, f32[2048]{0:T(1024)S(1)}, f32[2048]{0:T(1024)S(1)}, /*index=5*/f32[2...) fusion(f32[512]{0:T(512)S(1)} %bitcast.135, ...), kind=kLoop, calls=%fused_computation.28.clone.1 | loop fusion | flops 57640960 | bytes 161792 | tf_op jit(solution)/shard_map/while/body/eval_jaxpr/reduce_sum | solution.py:40
  250.9 11.7 %fusion.58 = (f32[2048]{0:T(1024)S(1)}, f32[2048]{0:T(1024)S(1)}, f32[2048]{0:T(1024)S(1)}, f32[2048]{0:T(1024)S(1)}, f32[2048]{0:T(1024)S(1)}, /*index=5*/f32[2...) fusion(f32[512]{0:T(512)S(1)} %bitcast.135, ...), kind=kLoop, calls=%fused_computation.28.clone.1 | loop fusion | flops 57640960 | bytes 161792 | tf_op jit(solution)/shard_map/while/body/eval_jaxpr/reduce_sum | solution.py:40
  266.0 11.7 %fusion.58 = (f32[2048]{0:T(1024)S(1)}, f32[2048]{0:T(1024)S(1)}, f32[2048]{0:T(1024)S(1)}, f32[2048]{0:T(1024)S(1)}, f32[2048]{0:T(1024)S(1)}, /*index=5*/f32[2...) fusion(f32[512]{0:T(512)S(1)} %bitcast.135, ...), kind=kLoop, calls=%fused_computation.28.clone.1 | loop fusion | flops 57640960 | bytes 161792 | tf_op jit(solution)/shard_map/while/body/eval_jaxpr/reduce_sum | solution.py:40
  278.0 1.4 copy.86
  279.6 634.6 %reduce-scatter.4.cloned.1.call-done = f32[16,15]{1,0:T(8,128)} async-done(((f32[2048,15]{1,0:T(8,128)}), f32[16,15]{1,0:T(8,128)}) %reduce-scatter.4.cloned.1.call-update) | async-done | bytes 976
  914.2 1.7 fusion.33
  (123 shorter events, 47.1 us)
Async XLA Ops:
  9.4 24.9 %all-to-all-start = ((f32[128,8,8]{1,2,0:T(8,128)}), f32[128,8,8]{1,2,0:T(8,128)S(1)}, u32[]{:S(2)}, u32[]{:S(2)}) async-start(f32[128,8,8]{1,2,0:T(8,128)} %stack.36), calls=%async_computation | async-start | bytes 1048576 | tf_op jit(solution)/shard_map/all_to_all | solution.py:109
  20.5 893.7 %reduce-scatter.4.cloned.1.call-start = ((), (), s32[]{:S(2)}) async-start(), calls=%async_computation.2 | async-start | bytes 1056768
Sparse Core Ops, SparseCore 0:
  279.5 634.6 reduce-scatter.3
